TPU v7x, 512 devices: a whole 4x8x8 slice. The times are simulated.
512 devices in a mesh: ctx: 32 (over z, x), exp: 16 (over y, core).
Axes of the slice: x: 4, y: 8, z: 8, core: 2. Of those that a mesh axis runs over, the one named last changes fastest.
Arguments:
- stream: bfloat16 [16, 4096, 1024], P('exp', 'ctx'), may hold values from -400 to 400
- queries: bfloat16 [16, 4096, 16, 128], P('exp', 'ctx'), may hold values from -6 to 6
- key_rows: bfloat16 [16, 4096, 2, 128], P('exp', 'ctx'), may hold values from -4 to 4
- value_rows: bfloat16 [16, 4096, 2, 128], P('exp', 'ctx'), may hold values from -6 to 6
- expert_ids: int32 [16, 4096, 2], P('exp', 'ctx'), may hold values from 0 to 127, as said below
- norm_gain: bfloat16 [1024], replicated, may hold values from 0.099609375 to 1.8984375
- router_weight: bfloat16 [1024, 128], replicated, may hold values from -0.1875 to 0.1875
- gate_weight: bfloat16 [98304, 1024], P(('ctx', 'exp')), may hold values from -0.1875 to 0.1875
- up_weight: bfloat16 [98304, 1024], P(('ctx', 'exp')), may hold values from -0.1875 to 0.1875
- down_weight: bfloat16 [98304, 1024], P(('ctx', 'exp')), may hold values from -0.21875 to 0.21875
Outputs:
- attended: bfloat16 [16, 4096, 16, 128], P('exp', 'ctx')
- expert_mix: bfloat16 [16, 4096, 1024], P('exp', 'ctx')
Inputs may be any that keep to these rules, and one draw needn't show every extreme that they name: `expert_ids`: within the rows of one device (aligned blocks of 128 positions of one sequence), a token's 2 experts differ and no expert is named more than 4 times; one expert is named exactly 4 times in every such block.
All inputs are finite; a program needn't handle non-finite values.
Results may differ from a plain program's by a relative error of at most 0.01.
Values may be sent and summed in bfloat16 or wider, within the bound.
No kernel may reach another device: no remote copies, remote signals or barrier semaphores. Data moves between devices by JAX's collectives and lax.ppermute only.
A program may use at most 64 MiB of HBM per device.

v0:
```python
import math
import jax
import jax.numpy as jnp
from jax import lax
from jax.sharding import PartitionSpec as P


def from_partner(value, axis, bit):
    return lax.ppermute(value, axis, [(i, i ^ 1 << bit) for i in range(lax.axis_size(axis))])


def expert_rows(inputs, gate_rows, up_rows, down_rows):
    features = inputs.shape[-1]
    flat_rows = inputs.reshape(-1, features)
    contract = (((1,), (1,)), ((), ()))
    gate_part = lax.dot_general(flat_rows, gate_rows, contract, preferred_element_type=jnp.float32)
    up_part = lax.dot_general(flat_rows, up_rows, contract, preferred_element_type=jnp.float32)
    hidden = (jax.nn.silu(gate_part) * up_part).astype(jnp.bfloat16)
    projected = jnp.dot(hidden, down_rows, preferred_element_type=jnp.float32)
    return projected.reshape(inputs.shape)


def attention(queries, key_rows, value_rows):
    seq_rows = queries.shape[1]
    head_count = queries.shape[2]
    head_size = queries.shape[3]
    kv_count = key_rows.shape[2]
    group_size = head_count // kv_count
    grouped = queries[0].reshape(seq_rows, kv_count, group_size, head_size)
    scaling = 1.0 / math.sqrt(head_size)
    query_pos = lax.axis_index("ctx") * seq_rows + jnp.arange(seq_rows, dtype=jnp.int32)
    initial = (
        jnp.full((kv_count, group_size, seq_rows), -1e30, jnp.float32),
        jnp.zeros((kv_count, group_size, seq_rows), jnp.float32),
        jnp.zeros((kv_count, group_size, seq_rows, head_size), jnp.float32),
    )
    key_piece = lax.all_gather(key_rows, "ctx", axis=1, tiled=True)
    value_piece = lax.all_gather(value_rows, "ctx", axis=1, tiled=True)
    piece_rows = key_piece.shape[1]
    block_rows = math.gcd(piece_rows, 512)
    block_count = piece_rows // block_rows
    key_blocks = key_piece[0].reshape(block_count, block_rows, kv_count, head_size)
    value_blocks = value_piece[0].reshape(block_count, block_rows, kv_count, head_size)

    def advance(status, members):
        running, totals, accumulated = status
        key_block, value_block, offset = members
        scores = (
            jnp.einsum("qhgd,khd->hgqk", grouped, key_block, preferred_element_type=jnp.float32)
            * scaling
        )
        key_pos = offset * block_rows + jnp.arange(block_rows, dtype=jnp.int32)
        visible = key_pos[None, :] <= query_pos[:, None]
        scores = jnp.where(visible, scores, -1e30)
        highest = jnp.maximum(running, jnp.max(scores, axis=-1))
        factor = jnp.exp(running - highest)
        weights = jnp.where(visible, jnp.exp(scores - highest[..., None]), 0.0)
        totals = totals * factor + jnp.sum(weights, axis=-1)
        accumulated = accumulated * factor[..., None] + jnp.einsum(
            "hgqk,khd->hgqd",
            weights.astype(jnp.bfloat16),
            value_block,
            preferred_element_type=jnp.float32,
        )
        return ((highest, totals, accumulated), None)

    status, unused = lax.scan(
        advance, initial, (key_blocks, value_blocks, jnp.arange(block_count, dtype=jnp.int32))
    )
    running, totals, accumulated = status
    result = accumulated / totals[..., None]
    return (
        jnp.transpose(result, (2, 0, 1, 3))
        .reshape(1, seq_rows, head_count, head_size)
        .astype(jnp.bfloat16)
    )


def local(
    stream,
    queries,
    key_rows,
    value_rows,
    expert_ids,
    norm_gain,
    router_weight,
    gate_weight,
    up_weight,
    down_weight,
):
    attended = attention(queries, key_rows, value_rows)
    ctx_count = lax.axis_size("ctx")
    exp_count = lax.axis_size("exp")
    tokens = stream.shape[1]
    features = stream.shape[2]
    top_count = expert_ids.shape[2]
    expert_total = router_weight.shape[1]
    per_ctx = expert_total // ctx_count
    quarters = exp_count // per_ctx
    capacity = 2 * tokens * top_count // expert_total
    widened = stream[0].astype(jnp.float32)
    mean_square = jnp.mean(widened * widened, axis=-1, keepdims=True)
    normed = (widened * lax.rsqrt(mean_square + 1e-06) * norm_gain.astype(jnp.float32)).astype(
        jnp.bfloat16
    )
    logits = jnp.dot(normed, router_weight, preferred_element_type=jnp.float32)
    chosen = expert_ids[0]
    gate_values = jax.nn.sigmoid(jnp.take_along_axis(logits, chosen, axis=1))
    flat_ids = chosen.reshape(-1)
    onehot = (flat_ids[:, None] == jnp.arange(expert_total, dtype=jnp.int32)[None, :]).astype(
        jnp.int32
    )
    earlier = jnp.cumsum(onehot, axis=0) - onehot
    slot_index = jnp.sum(earlier * onehot, axis=1)
    target = (flat_ids % per_ctx * ctx_count + flat_ids // per_ctx) * capacity + slot_index
    source_rows = jnp.repeat(normed, top_count, axis=0)
    outgoing = (
        jnp.zeros((expert_total * capacity, features), jnp.bfloat16).at[target].set(source_rows)
    )
    outgoing = outgoing.reshape(per_ctx, ctx_count, capacity, features)
    arrived = lax.all_to_all(outgoing, "ctx", split_axis=1, concat_axis=1, tiled=True)
    stacked = jnp.stack([gate_weight, up_weight, down_weight], axis=0)
    my_exp = lax.axis_index("exp")
    partner = from_partner(stacked, "exp", 0)
    upper_side = my_exp & 1 == 1
    held = jnp.where(
        upper_side,
        jnp.concatenate([partner, stacked], axis=1),
        jnp.concatenate([stacked, partner], axis=1),
    )
    half_ctx = ctx_count // 2
    halves_rows = arrived.reshape(per_ctx, 1, 2, half_ctx, capacity, features)
    spread_rows = jnp.broadcast_to(
        halves_rows, (per_ctx, quarters // 2, 2, half_ctx, capacity, features)
    )
    spread_rows = spread_rows.reshape(exp_count, half_ctx, capacity, features)
    received = lax.all_to_all(spread_rows, "exp", split_axis=0, concat_axis=0, tiled=True)
    partials = expert_rows(received, held[0], held[1], held[2])
    returned = lax.all_to_all(
        partials.astype(jnp.bfloat16), "exp", split_axis=0, concat_axis=0, tiled=True
    ).astype(partials.dtype)
    summed = jnp.sum(
        returned.reshape(per_ctx, quarters // 2, 2, half_ctx, capacity, features), axis=1
    )
    finished = summed.astype(jnp.bfloat16).reshape(per_ctx, ctx_count, capacity, features)
    came_back = lax.all_to_all(finished, "ctx", split_axis=1, concat_axis=1, tiled=True)
    flat_back = came_back.reshape(expert_total * capacity, features)
    picked = (
        jnp.take(flat_back, target, axis=0).astype(jnp.float32).reshape(tokens, top_count, features)
    )
    mixture = jnp.sum(picked * gate_values[:, :, None], axis=1).astype(jnp.bfloat16)
    return (attended, mixture[None])


def solution(mesh):
    placed = (
        P("exp", "ctx", None),
        P("exp", "ctx", None, None),
        P("exp", "ctx", None, None),
        P("exp", "ctx", None, None),
        P("exp", "ctx", None),
        P(),
        P(),
        P(("ctx", "exp"), None),
        P(("ctx", "exp"), None),
        P(("ctx", "exp"), None),
    )
    return jax.shard_map(
        local,
        mesh=mesh,
        in_specs=placed,
        out_specs=(P("exp", "ctx", None, None), P("exp", "ctx", None)),
        check_vma=False,
    )
```

profile of v0, /device:TPU:16, one launch (start us, length us, event | category | flops | bytes accessed | tf_op | source)
XLA Modules:
  0.0 309.8 jit_solution(2212090198150793443)
XLA Ops:
  12.4 1.9 scatter_custom_fusion
  16.4 13.2 %all-to-all-start = ((bf16[4,32,4,1024]{3,2,0,1:T(4,128)(2,1)}), bf16[4,32,4,1024]{3,2,0,1:T(4,128)(2,1)S(1)}, u32[]{:S(2)}, u32[]{:S(2)}) async-start(bf16[4,32,4,1024]{3,2,0,1:T(4,128)(2,1)} %copy.84), calls=%async_computation | async-start | bytes 2097152 | tf_op jit(solution)/shard_map/all_to_all | solution.py:121
  30.3 27.4 %all-to-all-done = bf16[4,32,4,1024]{3,2,0,1:T(4,128)(2,1)S(1)} async-done(((bf16[4,32,4,1024]{3,2,0,1:T(4,128)(2,1)}), bf16[4,32,4,1024]{3,2,0,1:T(4,128)(2,1)S(1)}, u32[]{:S(2)}, u32[]{:S(2)}) %all-to-all-start) | async-done | bytes 1048608 | tf_op jit(solution)/shard_map/all_to_all | solution.py:121
  58.1 2.1 broadcast_in_dim.66
  60.2 7.6 %all-to-all-start.1 = ((bf16[16,16,4,1024]{3,2,1,0:T(4,128)(2,1)}), bf16[16,16,4,1024]{3,2,1,0:T(4,128)(2,1)S(1)}, u32[]{:S(2)}, u32[]{:S(2)}) async-start(bf16[16,16,4,1024]{3,2,1,0:T(4,128)(2,1)} %bitcast.120), calls=%async_computation.1 | async-start | bytes 4194304 | tf_op jit(solution)/shard_map/all_to_all | solution.py:137
  67.8 2.2 pad_maximum_fusion
  70.0 2.0 collective-permute-start
  72.7 2.3 collective-permute-done
  75.1 3.5 %maximum_select_fusion = bf16[3,384,1024]{2,1,0:T(8,128)(2,1)} fusion(bf16[1,192,1024]{2,1,0:T(8,128)(2,1)S(1)} %bitcast.124, bf16[1,192,1024]{2,1,0:T(8,128)(2,1)S(1)} %bitcast.126, bf16[1,192,1024]{2,1,0:T(8,128)(2,1)} %bitcast.128, bf16[3,192,1024]{2,1,0:T(8,128)(2,1)} %collective-permute-done, pred[]{:T(512)S(6)} %eq.35), kind=kLoop, calls=%fused_computation.30 | loop fusion | flops 20054016 | bytes 4718593 | tf_op jit(solution)/shard_map/jit(_where)/select_n | solution.py:126
  78.6 36.6 %all-to-all-done.1 = bf16[16,16,4,1024]{3,2,1,0:T(4,128)(2,1)S(1)} async-done(((bf16[16,16,4,1024]{3,2,1,0:T(4,128)(2,1)}), bf16[16,16,4,1024]{3,2,1,0:T(4,128)(2,1)S(1)}, u32[]{:S(2)}, u32[]{:S(2)}) %all-to-all-start.1) | async-done | bytes 2097184 | tf_op jit(solution)/shard_map/all_to_all | solution.py:137
  115.2 2.0 reshape.284
  117.2 3.2 %fusion.22 = f32[1024,384]{1,0:T(8,128)S(1)} fusion(bf16[1024,1024]{1,0:T(8,128)(2,1)} %reshape.284, bf16[3,384,1024]{2,1,0:T(8,128)(2,1)} %maximum_select_fusion), kind=kOutput, calls=%fused_computation.40 | convolution fusion | flops 805306368 | bytes 4456448 | tf_op jit(solution)/shard_map/dot_general | solution.py:16
  120.4 2.3 multiply_convert_fusion
  122.7 2.4 dot_general.22
  125.1 3.7 %convolution_convert_fusion = bf16[16,16,4,1024]{3,1,2,0:T(8,128)(2,1)} fusion(bf16[3,384,1024]{2,1,0:T(8,128)(2,1)S(1)} %copy-done.2, bf16[16,16,4,384]{3,2,1,0:T(4,128)(2,1)} %dot_general.22), kind=kOutput, calls=%fused_computation.31 | convolution fusion | flops 806354944 | bytes 3670016 | tf_op jit(solution)/shard_map/dot_general | solution.py:19
  128.8 6.7 %all-to-all-start.2 = ((bf16[16,16,4,1024]{3,1,2,0:T(8,128)(2,1)}), bf16[16,16,4,1024]{3,1,2,0:T(8,128)(2,1)S(1)}, u32[]{:S(2)}, u32[]{:S(2)}) async-start(bf16[16,16,4,1024]{3,1,2,0:T(8,128)(2,1)} %convolution_convert_fusion), calls=%async_computation.2 | async-start | bytes 4194304 | tf_op jit(solution)/shard_map/all_to_all | solution.py:139
  137.6 1.9 gather_fusion.1
  139.9 43.0 %all-to-all-done.2 = bf16[16,16,4,1024]{3,1,2,0:T(8,128)(2,1)S(1)} async-done(((bf16[16,16,4,1024]{3,1,2,0:T(8,128)(2,1)}), bf16[16,16,4,1024]{3,1,2,0:T(8,128)(2,1)S(1)}, u32[]{:S(2)}, u32[]{:S(2)}) %all-to-all-start.2) | async-done | bytes 2097184 | tf_op jit(solution)/shard_map/all_to_all | solution.py:139
  182.8 1.8 reduce
  185.9 1.8 copy.88
  187.7 5.3 %all-to-all-start.3 = ((bf16[4,32,4,1024]{3,2,0,1:T(4,128)(2,1)}), bf16[4,32,4,1024]{3,2,0,1:T(4,128)(2,1)S(1)}, u32[]{:S(2)}, u32[]{:S(2)}) async-start(bf16[4,32,4,1024]{3,2,0,1:T(4,128)(2,1)} %copy.88), calls=%async_computation.3 | async-start | bytes 2097152 | tf_op jit(solution)/shard_map/all_to_all | solution.py:146
  193.1 14.3 %all-gather.5.cloned.1.call-done = bf16[1,4096,2,128]{3,1,2,0:T(8,128)(2,1)} async-done(((bf16[1,128,2,128]{3,1,2,0:T(8,128)(2,1)}), bf16[1,4096,2,128]{3,1,2,0:T(8,128)(2,1)}) %all-gather.5.cloned.1.call-update) | async-done | bytes 2097168 | tf_op jit(solution)/shard_map/all_gather | solution.py:38
  207.4 89.6 %while.15 = (s32[]{:T(128)}, f32[2,8,128]{2,1,0:T(8,128)S(1)}, f32[2,8,128]{2,1,0:T(8,128)S(1)}, f32[2,8,128,128]{3,2,1,0:T(8,128)S(1)}, s32[8]{0:T(128)S(1)}, /...) while((s32[]{:T(128)}, f32[2,8,128]{2,1,0:T(8,128)S(1)}, ...), condition=%wide.region_3.4_spmd.clone, body=%wide.region_0.3_spmd.clone.sunk | while | flops 551365248 | bytes 32904396 | solution.py:67
  208.8 3.7 %fusion.58 = (f32[2,8,128]{2,1,0:T(8,128)S(1)}, f32[2,512,128,8]{2,1,3,0:T(8,128)}) fusion(pred[128,512]{0,1:T(8,128)(4,1)S(1)} %broadcast_compare_fusion.2, bf16[128,2,8,128]{3,0,2,1:T(8,128)(2,1)S(1)} %get-tuple-element.236, bf16[8,512,2,128]{3,1,0,2:T(8,128)(2,1)} %get-tuple-element.235, s32[]{:T(128)S(6)} %copy.107), kind=kOutput, calls=%fused_computation.6.clone.1 | convolution fusion | flops 271579136 | bytes 5054468 | tf_op jit(solution)/shard_map/while/body/eval_jaxpr/qhgd,khd->hgqk/dot_general | solution.py:49
  212.5 3.3 %fusion.59 = f32[2,8,128]{2,1,0:T(8,128)S(1)} fusion(f32[2,512,128,8]{2,1,3,0:T(8,128)} %get-tuple-element.203, f32[2,8,128]{2,1,0:T(8,128)S(1)} %select_maximum_fusion.2, pred[128,512]{0,1:T(8,128)(4,1)S(1)} %broadcast_compare_fusion.2), kind=kLoop, calls=%fused_computation.8.clone.1 | loop fusion | flops 5240832 | bytes 4276224 | tf_op jit(solution)/shard_map/while/body/eval_jaxpr/reduce_sum | solution.py:58
  216.0 2.6 fusion.61
  220.0 3.7 %fusion.58 = (f32[2,8,128]{2,1,0:T(8,128)S(1)}, f32[2,512,128,8]{2,1,3,0:T(8,128)}) fusion(pred[128,512]{0,1:T(8,128)(4,1)S(1)} %broadcast_compare_fusion.2, bf16[128,2,8,128]{3,0,2,1:T(8,128)(2,1)S(1)} %get-tuple-element.236, bf16[8,512,2,128]{3,1,0,2:T(8,128)(2,1)} %get-tuple-element.235, s32[]{:T(128)S(6)} %copy.107), kind=kOutput, calls=%fused_computation.6.clone.1 | convolution fusion | flops 271579136 | bytes 5054468 | tf_op jit(solution)/shard_map/while/body/eval_jaxpr/qhgd,khd->hgqk/dot_general | solution.py:49
  223.7 3.3 %fusion.59 = f32[2,8,128]{2,1,0:T(8,128)S(1)} fusion(f32[2,512,128,8]{2,1,3,0:T(8,128)} %get-tuple-element.203, f32[2,8,128]{2,1,0:T(8,128)S(1)} %select_maximum_fusion.2, pred[128,512]{0,1:T(8,128)(4,1)S(1)} %broadcast_compare_fusion.2), kind=kLoop, calls=%fused_computation.8.clone.1 | loop fusion | flops 5240832 | bytes 4276224 | tf_op jit(solution)/shard_map/while/body/eval_jaxpr/reduce_sum | solution.py:58
  227.2 2.6 fusion.61
  231.2 3.7 %fusion.58 = (f32[2,8,128]{2,1,0:T(8,128)S(1)}, f32[2,512,128,8]{2,1,3,0:T(8,128)}) fusion(pred[128,512]{0,1:T(8,128)(4,1)S(1)} %broadcast_compare_fusion.2, bf16[128,2,8,128]{3,0,2,1:T(8,128)(2,1)S(1)} %get-tuple-element.236, bf16[8,512,2,128]{3,1,0,2:T(8,128)(2,1)} %get-tuple-element.235, s32[]{:T(128)S(6)} %copy.107), kind=kOutput, calls=%fused_computation.6.clone.1 | convolution fusion | flops 271579136 | bytes 5054468 | tf_op jit(solution)/shard_map/while/body/eval_jaxpr/qhgd,khd->hgqk/dot_general | solution.py:49
  234.9 3.3 %fusion.59 = f32[2,8,128]{2,1,0:T(8,128)S(1)} fusion(f32[2,512,128,8]{2,1,3,0:T(8,128)} %get-tuple-element.203, f32[2,8,128]{2,1,0:T(8,128)S(1)} %select_maximum_fusion.2, pred[128,512]{0,1:T(8,128)(4,1)S(1)} %broadcast_compare_fusion.2), kind=kLoop, calls=%fused_computation.8.clone.1 | loop fusion | flops 5240832 | bytes 4276224 | tf_op jit(solution)/shard_map/while/body/eval_jaxpr/reduce_sum | solution.py:58
  238.4 2.6 fusion.61
  242.5 3.7 %fusion.58 = (f32[2,8,128]{2,1,0:T(8,128)S(1)}, f32[2,512,128,8]{2,1,3,0:T(8,128)}) fusion(pred[128,512]{0,1:T(8,128)(4,1)S(1)} %broadcast_compare_fusion.2, bf16[128,2,8,128]{3,0,2,1:T(8,128)(2,1)S(1)} %get-tuple-element.236, bf16[8,512,2,128]{3,1,0,2:T(8,128)(2,1)} %get-tuple-element.235, s32[]{:T(128)S(6)} %copy.107), kind=kOutput, calls=%fused_computation.6.clone.1 | convolution fusion | flops 271579136 | bytes 5054468 | tf_op jit(solution)/shard_map/while/body/eval_jaxpr/qhgd,khd->hgqk/dot_general | solution.py:49
  246.1 3.3 %fusion.59 = f32[2,8,128]{2,1,0:T(8,128)S(1)} fusion(f32[2,512,128,8]{2,1,3,0:T(8,128)} %get-tuple-element.203, f32[2,8,128]{2,1,0:T(8,128)S(1)} %select_maximum_fusion.2, pred[128,512]{0,1:T(8,128)(4,1)S(1)} %broadcast_compare_fusion.2), kind=kLoop, calls=%fused_computation.8.clone.1 | loop fusion | flops 5240832 | bytes 4276224 | tf_op jit(solution)/shard_map/while/body/eval_jaxpr/reduce_sum | solution.py:58
  249.6 2.6 fusion.61
  253.7 3.7 %fusion.58 = (f32[2,8,128]{2,1,0:T(8,128)S(1)}, f32[2,512,128,8]{2,1,3,0:T(8,128)}) fusion(pred[128,512]{0,1:T(8,128)(4,1)S(1)} %broadcast_compare_fusion.2, bf16[128,2,8,128]{3,0,2,1:T(8,128)(2,1)S(1)} %get-tuple-element.236, bf16[8,512,2,128]{3,1,0,2:T(8,128)(2,1)} %get-tuple-element.235, s32[]{:T(128)S(6)} %copy.107), kind=kOutput, calls=%fused_computation.6.clone.1 | convolution fusion | flops 271579136 | bytes 5054468 | tf_op jit(solution)/shard_map/while/body/eval_jaxpr/qhgd,khd->hgqk/dot_general | solution.py:49
  257.3 3.3 %fusion.59 = f32[2,8,128]{2,1,0:T(8,128)S(1)} fusion(f32[2,512,128,8]{2,1,3,0:T(8,128)} %get-tuple-element.203, f32[2,8,128]{2,1,0:T(8,128)S(1)} %select_maximum_fusion.2, pred[128,512]{0,1:T(8,128)(4,1)S(1)} %broadcast_compare_fusion.2), kind=kLoop, calls=%fused_computation.8.clone.1 | loop fusion | flops 5240832 | bytes 4276224 | tf_op jit(solution)/shard_map/while/body/eval_jaxpr/reduce_sum | solution.py:58
  260.8 2.6 fusion.61
  264.9 3.7 %fusion.58 = (f32[2,8,128]{2,1,0:T(8,128)S(1)}, f32[2,512,128,8]{2,1,3,0:T(8,128)}) fusion(pred[128,512]{0,1:T(8,128)(4,1)S(1)} %broadcast_compare_fusion.2, bf16[128,2,8,128]{3,0,2,1:T(8,128)(2,1)S(1)} %get-tuple-element.236, bf16[8,512,2,128]{3,1,0,2:T(8,128)(2,1)} %get-tuple-element.235, s32[]{:T(128)S(6)} %copy.107), kind=kOutput, calls=%fused_computation.6.clone.1 | convolution fusion | flops 271579136 | bytes 5054468 | tf_op jit(solution)/shard_map/while/body/eval_jaxpr/qhgd,khd->hgqk/dot_general | solution.py:49
  268.6 3.3 %fusion.59 = f32[2,8,128]{2,1,0:T(8,128)S(1)} fusion(f32[2,512,128,8]{2,1,3,0:T(8,128)} %get-tuple-element.203, f32[2,8,128]{2,1,0:T(8,128)S(1)} %select_maximum_fusion.2, pred[128,512]{0,1:T(8,128)(4,1)S(1)} %broadcast_compare_fusion.2), kind=kLoop, calls=%fused_computation.8.clone.1 | loop fusion | flops 5240832 | bytes 4276224 | tf_op jit(solution)/shard_map/while/body/eval_jaxpr/reduce_sum | solution.py:58
  272.0 2.6 fusion.61
  276.1 3.7 %fusion.58 = (f32[2,8,128]{2,1,0:T(8,128)S(1)}, f32[2,512,128,8]{2,1,3,0:T(8,128)}) fusion(pred[128,512]{0,1:T(8,128)(4,1)S(1)} %broadcast_compare_fusion.2, bf16[128,2,8,128]{3,0,2,1:T(8,128)(2,1)S(1)} %get-tuple-element.236, bf16[8,512,2,128]{3,1,0,2:T(8,128)(2,1)} %get-tuple-element.235, s32[]{:T(128)S(6)} %copy.107), kind=kOutput, calls=%fused_computation.6.clone.1 | convolution fusion | flops 271579136 | bytes 5054468 | tf_op jit(solution)/shard_map/while/body/eval_jaxpr/qhgd,khd->hgqk/dot_general | solution.py:49
  279.8 3.3 %fusion.59 = f32[2,8,128]{2,1,0:T(8,128)S(1)} fusion(f32[2,512,128,8]{2,1,3,0:T(8,128)} %get-tuple-element.203, f32[2,8,128]{2,1,0:T(8,128)S(1)} %select_maximum_fusion.2, pred[128,512]{0,1:T(8,128)(4,1)S(1)} %broadcast_compare_fusion.2), kind=kLoop, calls=%fused_computation.8.clone.1 | loop fusion | flops 5240832 | bytes 4276224 | tf_op jit(solution)/shard_map/while/body/eval_jaxpr/reduce_sum | solution.py:58
  283.2 2.6 fusion.61
  287.3 3.7 %fusion.58 = (f32[2,8,128]{2,1,0:T(8,128)S(1)}, f32[2,512,128,8]{2,1,3,0:T(8,128)}) fusion(pred[128,512]{0,1:T(8,128)(4,1)S(1)} %broadcast_compare_fusion.2, bf16[128,2,8,128]{3,0,2,1:T(8,128)(2,1)S(1)} %get-tuple-element.236, bf16[8,512,2,128]{3,1,0,2:T(8,128)(2,1)} %get-tuple-element.235, s32[]{:T(128)S(6)} %copy.107), kind=kOutput, calls=%fused_computation.6.clone.1 | convolution fusion | flops 271579136 | bytes 5054468 | tf_op jit(solution)/shard_map/while/body/eval_jaxpr/qhgd,khd->hgqk/dot_general | solution.py:49
  291.0 3.3 %fusion.59 = f32[2,8,128]{2,1,0:T(8,128)S(1)} fusion(f32[2,512,128,8]{2,1,3,0:T(8,128)} %get-tuple-element.203, f32[2,8,128]{2,1,0:T(8,128)S(1)} %select_maximum_fusion.2, pred[128,512]{0,1:T(8,128)(4,1)S(1)} %broadcast_compare_fusion.2), kind=kLoop, calls=%fused_computation.8.clone.1 | loop fusion | flops 5240832 | bytes 4276224 | tf_op jit(solution)/shard_map/while/body/eval_jaxpr/reduce_sum | solution.py:58
  294.4 2.6 fusion.61
  300.6 2.3 multiply_reduce_fusion
  (146 shorter events, 23.0 us)
Async XLA Ops:
  7.2 130.2 %copy-start = (bf16[1024,128]{1,0:T(8,128)(2,1)S(1)}, bf16[1024,128]{1,0:T(8,128)(2,1)}, u32[]{:S(2)}) copy-start(bf16[1024,128]{1,0:T(8,128)(2,1)} %param.18) | copy-start | bytes 786436
  14.8 14.8 %copy-start.7 = (bf16[1,128,2,128]{3,2,1,0:T(2,128)(2,1)S(1)}, bf16[1,128,2,128]{3,2,1,0:T(2,128)(2,1)}, u32[]{:S(2)}) copy-start(bf16[1,128,2,128]{3,2,1,0:T(2,128)(2,1)} %param.14) | copy-start | bytes 196612
  16.4 41.3 %all-to-all-start = ((bf16[4,32,4,1024]{3,2,0,1:T(4,128)(2,1)}), bf16[4,32,4,1024]{3,2,0,1:T(4,128)(2,1)S(1)}, u32[]{:S(2)}, u32[]{:S(2)}) async-start(bf16[4,32,4,1024]{3,2,0,1:T(4,128)(2,1)} %copy.84), calls=%async_computation | async-start | bytes 2097152 | tf_op jit(solution)/shard_map/all_to_all | solution.py:121
  29.5 163.6 %all-gather.3.cloned.1.call-start = ((), (), s32[]{:S(2)}) async-start(), calls=%async_computation.4 | async-start | bytes 2162688 | tf_op jit(solution)/shard_map/all_gather | solution.py:37
  60.2 7.6 %copy-start.4 = (bf16[192,1024]{1,0:T(8,128)(2,1)S(1)}, bf16[192,1024]{1,0:T(8,128)(2,1)}, u32[]{:S(2)}) copy-start(bf16[192,1024]{1,0:T(8,128)(2,1)} %param.21) | copy-start | bytes 1179652
  60.2 7.6 %copy-start.5 = (bf16[192,1024]{1,0:T(8,128)(2,1)S(1)}, bf16[192,1024]{1,0:T(8,128)(2,1)}, u32[]{:S(2)}) copy-start(bf16[192,1024]{1,0:T(8,128)(2,1)} %param.20) | copy-start | bytes 1179652
  60.2 11.9 %copy-start.8 = (bf16[1,128,2,128]{3,2,1,0:T(2,128)(2,1)S(1)}, bf16[1,128,2,128]{3,2,1,0:T(2,128)(2,1)}, u32[]{:S(2)}) copy-start(bf16[1,128,2,128]{3,2,1,0:T(2,128)(2,1)} %param.15) | copy-start | bytes 196612
  60.2 55.0 %all-to-all-start.1 = ((bf16[16,16,4,1024]{3,2,1,0:T(4,128)(2,1)}), bf16[16,16,4,1024]{3,2,1,0:T(4,128)(2,1)S(1)}, u32[]{:S(2)}, u32[]{:S(2)}) async-start(bf16[16,16,4,1024]{3,2,1,0:T(4,128)(2,1)} %bitcast.120), calls=%async_computation.1 | async-start | bytes 4194304 | tf_op jit(solution)/shard_map/all_to_all | solution.py:137
  67.8 139.7 %all-gather.5.cloned.1.call-start = ((), (), s32[]{:S(2)}) async-start(), calls=%async_computation.5 | async-start | bytes 2162688 | tf_op jit(solution)/shard_map/all_gather | solution.py:38
  70.0 5.1 %collective-permute-start = (bf16[3,192,1024]{2,1,0:T(8,128)(2,1)}, bf16[3,192,1024]{2,1,0:T(8,128)(2,1)}, u32[]{:S(2)}, u32[]{:S(2)}) collective-permute-start(bf16[3,192,1024]{2,1,0:T(8,128)(2,1)} %pad_maximum_fusion), channel_id=1, source_target_pairs={{0,1},{1,0},{2,3},{3,2},{4,5},{5,4},{6,7},{7,6},{8,9},{9,8},{10,11... | collective-permute-start | bytes 3538952 | tf_op jit(solution)/shard_map/ppermute | solution.py:9
  117.2 3.2 %copy-start.2 = (bf16[3,384,1024]{2,1,0:T(8,128)(2,1)S(1)}, bf16[3,384,1024]{2,1,0:T(8,128)(2,1)}, u32[]{:S(2)}) copy-start(bf16[3,384,1024]{2,1,0:T(8,128)(2,1)} %maximum_select_fusion) | copy-start | bytes 7077892
  117.2 3.2 %copy-start.3 = (bf16[1024,1024]{1,0:T(8,128)(2,1)S(1)}, bf16[1024,1024]{1,0:T(8,128)(2,1)}, u32[]{:S(2)}) copy-start(bf16[1024,1024]{1,0:T(8,128)(2,1)} %reshape.284) | copy-start | bytes 6291460
  128.8 8.1 %copy-start.9 = (s32[1,128,2]{1,2,0:T(2,128)S(1)}, s32[1,128,2]{1,2,0:T(2,128)}, u32[]{:S(2)}) copy-start(s32[1,128,2]{1,2,0:T(2,128)} %param.16) | copy-start | bytes 3076
  128.8 54.1 %all-to-all-start.2 = ((bf16[16,16,4,1024]{3,1,2,0:T(8,128)(2,1)}), bf16[16,16,4,1024]{3,1,2,0:T(8,128)(2,1)S(1)}, u32[]{:S(2)}, u32[]{:S(2)}) async-start(bf16[16,16,4,1024]{3,1,2,0:T(8,128)(2,1)} %convolution_convert_fusion), calls=%async_computation.2 | async-start | bytes 4194304 | tf_op jit(solution)/shard_map/all_to_all | solution.py:139
  185.9 21.5 %copy-start.6 = (f32[2,8,128,128]{3,2,1,0:T(8,128)S(1)}, f32[2,8,128,128]{3,2,1,0:T(8,128)}, u32[]{:S(2)}) copy-start(f32[2,8,128,128]{3,2,1,0:T(8,128)} %custom-call.4) | copy-start | bytes 3145732
  187.7 110.8 %all-to-all-start.3 = ((bf16[4,32,4,1024]{3,2,0,1:T(4,128)(2,1)}), bf16[4,32,4,1024]{3,2,0,1:T(4,128)(2,1)S(1)}, u32[]{:S(2)}, u32[]{:S(2)}) async-start(bf16[4,32,4,1024]{3,2,0,1:T(4,128)(2,1)} %copy.88), calls=%async_computation.3 | async-start | bytes 2097152 | tf_op jit(solution)/shard_map/all_to_all | solution.py:146
  212.5 3.4 %copy-start.1 = (f32[2,512,128,8]{2,1,3,0:T(8,128)S(1)}, f32[2,512,128,8]{2,1,3,0:T(8,128)}, u32[]{:S(2)}) copy-start(f32[2,512,128,8]{2,1,3,0:T(8,128)} %get-tuple-element.203) | copy-start | bytes 12582916 | tf_op jit(solution)/shard_map/while
  223.7 3.4 %copy-start.1 = (f32[2,512,128,8]{2,1,3,0:T(8,128)S(1)}, f32[2,512,128,8]{2,1,3,0:T(8,128)}, u32[]{:S(2)}) copy-start(f32[2,512,128,8]{2,1,3,0:T(8,128)} %get-tuple-element.203) | copy-start | bytes 12582916 | tf_op jit(solution)/shard_map/while
  234.9 3.4 %copy-start.1 = (f32[2,512,128,8]{2,1,3,0:T(8,128)S(1)}, f32[2,512,128,8]{2,1,3,0:T(8,128)}, u32[]{:S(2)}) copy-start(f32[2,512,128,8]{2,1,3,0:T(8,128)} %get-tuple-element.203) | copy-start | bytes 12582916 | tf_op jit(solution)/shard_map/while
  246.1 3.4 %copy-start.1 = (f32[2,512,128,8]{2,1,3,0:T(8,128)S(1)}, f32[2,512,128,8]{2,1,3,0:T(8,128)}, u32[]{:S(2)}) copy-start(f32[2,512,128,8]{2,1,3,0:T(8,128)} %get-tuple-element.203) | copy-start | bytes 12582916 | tf_op jit(solution)/shard_map/while
  257.3 3.4 %copy-start.1 = (f32[2,512,128,8]{2,1,3,0:T(8,128)S(1)}, f32[2,512,128,8]{2,1,3,0:T(8,128)}, u32[]{:S(2)}) copy-start(f32[2,512,128,8]{2,1,3,0:T(8,128)} %get-tuple-element.203) | copy-start | bytes 12582916 | tf_op jit(solution)/shard_map/while
  268.5 3.4 %copy-start.1 = (f32[2,512,128,8]{2,1,3,0:T(8,128)S(1)}, f32[2,512,128,8]{2,1,3,0:T(8,128)}, u32[]{:S(2)}) copy-start(f32[2,512,128,8]{2,1,3,0:T(8,128)} %get-tuple-element.203) | copy-start | bytes 12582916 | tf_op jit(solution)/shard_map/while
  279.7 3.4 %copy-start.1 = (f32[2,512,128,8]{2,1,3,0:T(8,128)S(1)}, f32[2,512,128,8]{2,1,3,0:T(8,128)}, u32[]{:S(2)}) copy-start(f32[2,512,128,8]{2,1,3,0:T(8,128)} %get-tuple-element.203) | copy-start | bytes 12582916 | tf_op jit(solution)/shard_map/while
  290.9 3.4 %copy-start.1 = (f32[2,512,128,8]{2,1,3,0:T(8,128)S(1)}, f32[2,512,128,8]{2,1,3,0:T(8,128)}, u32[]{:S(2)}) copy-start(f32[2,512,128,8]{2,1,3,0:T(8,128)} %get-tuple-element.203) | copy-start | bytes 12582916 | tf_op jit(solution)/shard_map/while
Sparse Core Ops, SparseCore 0:
  34.1 84.8 all-gather.2
  122.8 84.6 all-gather.4
where the time goes:
time: 311 us; the launch traced here: 310 us
  waiting for transfers between devices  124 us (40%)
  matrix products  60 us (19%)
  other arithmetic  41.4 us (13%)
  starting transfers between devices  34.9 us (11%)
  local copies, waits for them, and re-layouts  29.7 us (10%)
  between operations  14.4 us (5%)
  loops' own time  5.69 us (2%)
    all_to_all x1, waiting for transfers between devices, local(): lax.all_to_all(partials.astype(jnp.bfloat16), 'exp', split_axis=0, concat...  43 us
    all_to_all x1, waiting for transfers between devices, local(): lax.all_to_all(spread_rows, 'exp', split_axis=0, concat_axis=0, tiled=True)  36.6 us
    dot_general x8, matrix products, advance(): jnp.einsum('qhgd,khd->hgqk', grouped, key_block, preferred_element_type=j...  29.5 us
    all_to_all x1, waiting for transfers between devices, local(): lax.all_to_all(outgoing, 'ctx', split_axis=1, concat_axis=1, tiled=True)  27.4 us
    reduce_sum x8, other arithmetic, advance(): totals = totals * factor + jnp.sum(weights, axis=-1)  26.6 us
    dot_general x8, matrix products, advance(): jnp.einsum('hgqk,khd->hgqd', weights.astype(jnp.bfloat16), value_block, p...  21.1 us
    all_gather x1, waiting for transfers between devices, attention(): value_piece = lax.all_gather(value_rows, 'ctx', axis=1, tiled=True)  14.3 us
    all_to_all x1, starting transfers between devices, local(): lax.all_to_all(outgoing, 'ctx', split_axis=1, concat_axis=1, tiled=True)  13.2 us
  transfers between devices with their start and end apart: 7, of which 5 were waited for; matrix products, arithmetic and copies ran while one was open for 38% of the time, Pallas kernels for 0%

commit v1 on v0

--- a/solution.py
+++ b/solution.py
@@ -118,7 +118,10 @@
         jnp.zeros((expert_total * capacity, features), jnp.bfloat16).at[target].set(source_rows)
     )
     outgoing = outgoing.reshape(per_ctx, ctx_count, capacity, features)
-    arrived = lax.all_to_all(outgoing, "ctx", split_axis=1, concat_axis=1, tiled=True)
+    arrived = jnp.concatenate(
+        lax.all_to_all(jnp.stack(jnp.split(outgoing, lax.axis_size("ctx"), axis=1)), "ctx", 0, 0),
+        axis=1,
+    )
     stacked = jnp.stack([gate_weight, up_weight, down_weight], axis=0)
     my_exp = lax.axis_index("exp")
     partner = from_partner(stacked, "exp", 0)

time: 311 us -> 329 us (1.058)
  the two profiles are of different devices: /device:TPU:16 before, /device:TPU:8 now
where the time goes in v1:
time: 329 us; the launch traced here: 327 us
  waiting for transfers between devices  123 us (37%)
  matrix products  59.4 us (18%)
  local copies, waits for them, and re-layouts  48.3 us (15%)
  other arithmetic  41.4 us (13%)
  starting transfers between devices  35 us (11%)
  between operations  14.4 us (4%)
  loops' own time  5.69 us (2%)
    all_to_all x1, waiting for transfers between devices, local(): lax.all_to_all(partials.astype(jnp.bfloat16), 'exp', split_axis=0, concat...  43 us
    all_to_all x1, waiting for transfers between devices, local(): lax.all_to_all(spread_rows, 'exp', split_axis=0, concat_axis=0, tiled=True)  36.6 us
    dot_general x8, matrix products, advance(): jnp.einsum('qhgd,khd->hgqk', grouped, key_block, preferred_element_type=j...  28.9 us
    all_to_all x1, waiting for transfers between devices, local(): lax.all_to_all(jnp.stack(jnp.split(outgoing, lax.axis_size('ctx'), axis=1...  27.4 us
    reduce_sum x8, other arithmetic, advance(): totals = totals * factor + jnp.sum(weights, axis=-1)  26.6 us
    unnamed x54, local copies, waits for them, and re-layouts  22.6 us
    dot_general x8, matrix products, advance(): jnp.einsum('hgqk,khd->hgqd', weights.astype(jnp.bfloat16), value_block, p...  21.1 us
    all_gather x1, waiting for transfers between devices, attention(): value_piece = lax.all_gather(value_rows, 'ctx', axis=1, tiled=True)  14 us
  transfers between devices with their start and end apart: 7, of which 5 were waited for; matrix products, arithmetic and copies ran while one was open for 36% of the time, Pallas kernels for 0%

profile of v1, /device:TPU:8, one launch (start us, length us, event | category | flops | bytes accessed | tf_op | source)
XLA Modules:
  0.0 327.4 jit_solution(14878235149718933328)
XLA Ops:
  12.4 1.9 scatter_custom_fusion
  34.7 13.2 %all-to-all-start = ((bf16[32,4,1,4,1024]{4,3,1,2,0:T(4,128)(2,1)}), bf16[32,4,1,4,1024]{4,3,1,2,0:T(4,128)(2,1)S(1)}, u32[]{:S(2)}, u32[]{:S(2)}) async-start(bf16[32,4,1,4,1024]{4,3,1,2,0:T(4,128)(2,1)} %constant_dynamic-update-slice_fusion), calls=%async_computation | async-start | bytes 2097152 | tf_op jit(solution)/shard_map/all_to_all | solution.py:122
  48.6 27.4 %all-to-all-done = bf16[32,4,1,4,1024]{4,3,1,2,0:T(4,128)(2,1)S(1)} async-done(((bf16[32,4,1,4,1024]{4,3,1,2,0:T(4,128)(2,1)}), bf16[32,4,1,4,1024]{4,3,1,2,0:T(4,128)(2,1)S(1)}, u32[]{:S(2)}, u32[]{:S(2)}) %all-to-all-start) | async-done | bytes 1048608 | tf_op jit(solution)/shard_map/all_to_all | solution.py:122
  76.4 2.2 broadcast_in_dim.66
  78.6 7.7 %all-to-all-start.1 = ((bf16[16,16,4,1024]{3,2,1,0:T(4,128)(2,1)}), bf16[16,16,4,1024]{3,2,1,0:T(4,128)(2,1)S(1)}, u32[]{:S(2)}, u32[]{:S(2)}) async-start(bf16[16,16,4,1024]{3,2,1,0:T(4,128)(2,1)} %bitcast.312), calls=%async_computation.1 | async-start | bytes 4194304 | tf_op jit(solution)/shard_map/all_to_all | solution.py:140
  86.4 2.1 pad_maximum_fusion
  88.5 2.0 collective-permute-start
  91.3 2.3 collective-permute-done
  93.6 3.5 %maximum_select_fusion = bf16[3,384,1024]{2,1,0:T(8,128)(2,1)} fusion(bf16[1,192,1024]{2,1,0:T(8,128)(2,1)S(1)} %bitcast.316, bf16[1,192,1024]{2,1,0:T(8,128)(2,1)S(1)} %bitcast.318, bf16[1,192,1024]{2,1,0:T(8,128)(2,1)} %bitcast.320, bf16[3,192,1024]{2,1,0:T(8,128)(2,1)} %collective-permute-done, pred[]{:T(512)S(6)} %eq.35), kind=kLoop, calls=%fused_computation.30 | loop fusion | flops 20054016 | bytes 4718593 | tf_op jit(solution)/shard_map/jit(_where)/select_n | solution.py:129
  97.1 36.6 %all-to-all-done.1 = bf16[16,16,4,1024]{3,2,1,0:T(4,128)(2,1)S(1)} async-done(((bf16[16,16,4,1024]{3,2,1,0:T(4,128)(2,1)}), bf16[16,16,4,1024]{3,2,1,0:T(4,128)(2,1)S(1)}, u32[]{:S(2)}, u32[]{:S(2)}) %all-to-all-start.1) | async-done | bytes 2097184 | tf_op jit(solution)/shard_map/all_to_all | solution.py:140
  133.7 2.1 reshape.287
  135.8 3.2 fusion.22
  139.0 2.2 multiply_convert_fusion
  141.2 2.4 dot_general.22
  143.6 3.7 %convolution_convert_fusion = bf16[16,16,4,1024]{3,1,2,0:T(8,128)(2,1)} fusion(bf16[3,384,1024]{2,1,0:T(8,128)(2,1)S(1)} %copy-done.2, bf16[16,16,4,384]{3,2,1,0:T(4,128)(2,1)} %dot_general.22), kind=kOutput, calls=%fused_computation.31 | convolution fusion | flops 806354944 | bytes 3670016 | tf_op jit(solution)/shard_map/dot_general | solution.py:19
  147.3 6.7 %all-to-all-start.2 = ((bf16[16,16,4,1024]{3,1,2,0:T(8,128)(2,1)}), bf16[16,16,4,1024]{3,1,2,0:T(8,128)(2,1)S(1)}, u32[]{:S(2)}, u32[]{:S(2)}) async-start(bf16[16,16,4,1024]{3,1,2,0:T(8,128)(2,1)} %convolution_convert_fusion), calls=%async_computation.2 | async-start | bytes 4194304 | tf_op jit(solution)/shard_map/all_to_all | solution.py:142
  156.1 1.9 gather_fusion.1
  158.4 43.0 %all-to-all-done.2 = bf16[16,16,4,1024]{3,1,2,0:T(8,128)(2,1)S(1)} async-done(((bf16[16,16,4,1024]{3,1,2,0:T(8,128)(2,1)}), bf16[16,16,4,1024]{3,1,2,0:T(8,128)(2,1)S(1)}, u32[]{:S(2)}, u32[]{:S(2)}) %all-to-all-start.2) | async-done | bytes 2097184 | tf_op jit(solution)/shard_map/all_to_all | solution.py:142
  201.4 1.8 reduce
  204.5 1.9 copy.243
  206.4 5.3 %all-to-all-start.3 = ((bf16[4,32,4,1024]{3,2,0,1:T(4,128)(2,1)}), bf16[4,32,4,1024]{3,2,0,1:T(4,128)(2,1)S(1)}, u32[]{:S(2)}, u32[]{:S(2)}) async-start(bf16[4,32,4,1024]{3,2,0,1:T(4,128)(2,1)} %copy.243), calls=%async_computation.3 | async-start | bytes 2097152 | tf_op jit(solution)/shard_map/all_to_all | solution.py:149
  211.7 14.0 %all-gather.5.cloned.1.call-done = bf16[1,4096,2,128]{3,1,2,0:T(8,128)(2,1)} async-done(((bf16[1,128,2,128]{3,1,2,0:T(8,128)(2,1)}), bf16[1,4096,2,128]{3,1,2,0:T(8,128)(2,1)}) %all-gather.5.cloned.1.call-update) | async-done | bytes 2097168 | tf_op jit(solution)/shard_map/all_gather | solution.py:38
  225.7 89.0 %while.15 = (s32[]{:T(128)}, f32[2,8,128]{2,1,0:T(8,128)S(1)}, f32[2,8,128]{2,1,0:T(8,128)S(1)}, f32[2,8,128,128]{3,2,1,0:T(8,128)S(1)}, s32[8]{0:T(128)S(1)}, /...) while((s32[]{:T(128)}, f32[2,8,128]{2,1,0:T(8,128)S(1)}, ...), condition=%wide.region_3.4_spmd.clone, body=%wide.region_0.3_spmd.clone.sunk | while | flops 551365248 | bytes 32904396 | solution.py:67
  227.1 3.6 %fusion.58 = (f32[2,8,128]{2,1,0:T(8,128)S(1)}, f32[2,512,128,8]{2,1,3,0:T(8,128)}) fusion(pred[128,512]{0,1:T(8,128)(4,1)S(1)} %broadcast_compare_fusion.2, bf16[128,2,8,128]{3,0,2,1:T(8,128)(2,1)S(1)} %get-tuple-element.236, bf16[8,512,2,128]{3,1,0,2:T(8,128)(2,1)} %get-tuple-element.235, s32[]{:T(128)S(6)} %copy.293), kind=kOutput, calls=%fused_computation.6.clone.1 | convolution fusion | flops 271579136 | bytes 5054468 | tf_op jit(solution)/shard_map/while/body/eval_jaxpr/qhgd,khd->hgqk/dot_general | solution.py:49
  230.7 3.3 %fusion.59 = f32[2,8,128]{2,1,0:T(8,128)S(1)} fusion(f32[2,512,128,8]{2,1,3,0:T(8,128)} %get-tuple-element.203, f32[2,8,128]{2,1,0:T(8,128)S(1)} %select_maximum_fusion.2, pred[128,512]{0,1:T(8,128)(4,1)S(1)} %broadcast_compare_fusion.2), kind=kLoop, calls=%fused_computation.8.clone.1 | loop fusion | flops 5240832 | bytes 4276224 | tf_op jit(solution)/shard_map/while/body/eval_jaxpr/reduce_sum | solution.py:58
  234.1 2.6 fusion.61
  238.2 3.6 %fusion.58 = (f32[2,8,128]{2,1,0:T(8,128)S(1)}, f32[2,512,128,8]{2,1,3,0:T(8,128)}) fusion(pred[128,512]{0,1:T(8,128)(4,1)S(1)} %broadcast_compare_fusion.2, bf16[128,2,8,128]{3,0,2,1:T(8,128)(2,1)S(1)} %get-tuple-element.236, bf16[8,512,2,128]{3,1,0,2:T(8,128)(2,1)} %get-tuple-element.235, s32[]{:T(128)S(6)} %copy.293), kind=kOutput, calls=%fused_computation.6.clone.1 | convolution fusion | flops 271579136 | bytes 5054468 | tf_op jit(solution)/shard_map/while/body/eval_jaxpr/qhgd,khd->hgqk/dot_general | solution.py:49
  241.8 3.3 %fusion.59 = f32[2,8,128]{2,1,0:T(8,128)S(1)} fusion(f32[2,512,128,8]{2,1,3,0:T(8,128)} %get-tuple-element.203, f32[2,8,128]{2,1,0:T(8,128)S(1)} %select_maximum_fusion.2, pred[128,512]{0,1:T(8,128)(4,1)S(1)} %broadcast_compare_fusion.2), kind=kLoop, calls=%fused_computation.8.clone.1 | loop fusion | flops 5240832 | bytes 4276224 | tf_op jit(solution)/shard_map/while/body/eval_jaxpr/reduce_sum | solution.py:58
  245.3 2.6 fusion.61
  249.3 3.6 %fusion.58 = (f32[2,8,128]{2,1,0:T(8,128)S(1)}, f32[2,512,128,8]{2,1,3,0:T(8,128)}) fusion(pred[128,512]{0,1:T(8,128)(4,1)S(1)} %broadcast_compare_fusion.2, bf16[128,2,8,128]{3,0,2,1:T(8,128)(2,1)S(1)} %get-tuple-element.236, bf16[8,512,2,128]{3,1,0,2:T(8,128)(2,1)} %get-tuple-element.235, s32[]{:T(128)S(6)} %copy.293), kind=kOutput, calls=%fused_computation.6.clone.1 | convolution fusion | flops 271579136 | bytes 5054468 | tf_op jit(solution)/shard_map/while/body/eval_jaxpr/qhgd,khd->hgqk/dot_general | solution.py:49
  253.0 3.3 %fusion.59 = f32[2,8,128]{2,1,0:T(8,128)S(1)} fusion(f32[2,512,128,8]{2,1,3,0:T(8,128)} %get-tuple-element.203, f32[2,8,128]{2,1,0:T(8,128)S(1)} %select_maximum_fusion.2, pred[128,512]{0,1:T(8,128)(4,1)S(1)} %broadcast_compare_fusion.2), kind=kLoop, calls=%fused_computation.8.clone.1 | loop fusion | flops 5240832 | bytes 4276224 | tf_op jit(solution)/shard_map/while/body/eval_jaxpr/reduce_sum | solution.py:58
  256.4 2.6 fusion.61
  260.5 3.6 %fusion.58 = (f32[2,8,128]{2,1,0:T(8,128)S(1)}, f32[2,512,128,8]{2,1,3,0:T(8,128)}) fusion(pred[128,512]{0,1:T(8,128)(4,1)S(1)} %broadcast_compare_fusion.2, bf16[128,2,8,128]{3,0,2,1:T(8,128)(2,1)S(1)} %get-tuple-element.236, bf16[8,512,2,128]{3,1,0,2:T(8,128)(2,1)} %get-tuple-element.235, s32[]{:T(128)S(6)} %copy.293), kind=kOutput, calls=%fused_computation.6.clone.1 | convolution fusion | flops 271579136 | bytes 5054468 | tf_op jit(solution)/shard_map/while/body/eval_jaxpr/qhgd,khd->hgqk/dot_general | solution.py:49
  264.1 3.3 %fusion.59 = f32[2,8,128]{2,1,0:T(8,128)S(1)} fusion(f32[2,512,128,8]{2,1,3,0:T(8,128)} %get-tuple-element.203, f32[2,8,128]{2,1,0:T(8,128)S(1)} %select_maximum_fusion.2, pred[128,512]{0,1:T(8,128)(4,1)S(1)} %broadcast_compare_fusion.2), kind=kLoop, calls=%fused_computation.8.clone.1 | loop fusion | flops 5240832 | bytes 4276224 | tf_op jit(solution)/shard_map/while/body/eval_jaxpr/reduce_sum | solution.py:58
  267.5 2.6 fusion.61
  271.6 3.6 %fusion.58 = (f32[2,8,128]{2,1,0:T(8,128)S(1)}, f32[2,512,128,8]{2,1,3,0:T(8,128)}) fusion(pred[128,512]{0,1:T(8,128)(4,1)S(1)} %broadcast_compare_fusion.2, bf16[128,2,8,128]{3,0,2,1:T(8,128)(2,1)S(1)} %get-tuple-element.236, bf16[8,512,2,128]{3,1,0,2:T(8,128)(2,1)} %get-tuple-element.235, s32[]{:T(128)S(6)} %copy.293), kind=kOutput, calls=%fused_computation.6.clone.1 | convolution fusion | flops 271579136 | bytes 5054468 | tf_op jit(solution)/shard_map/while/body/eval_jaxpr/qhgd,khd->hgqk/dot_general | solution.py:49
  275.2 3.3 %fusion.59 = f32[2,8,128]{2,1,0:T(8,128)S(1)} fusion(f32[2,512,128,8]{2,1,3,0:T(8,128)} %get-tuple-element.203, f32[2,8,128]{2,1,0:T(8,128)S(1)} %select_maximum_fusion.2, pred[128,512]{0,1:T(8,128)(4,1)S(1)} %broadcast_compare_fusion.2), kind=kLoop, calls=%fused_computation.8.clone.1 | loop fusion | flops 5240832 | bytes 4276224 | tf_op jit(solution)/shard_map/while/body/eval_jaxpr/reduce_sum | solution.py:58
  278.7 2.6 fusion.61
  282.7 3.6 %fusion.58 = (f32[2,8,128]{2,1,0:T(8,128)S(1)}, f32[2,512,128,8]{2,1,3,0:T(8,128)}) fusion(pred[128,512]{0,1:T(8,128)(4,1)S(1)} %broadcast_compare_fusion.2, bf16[128,2,8,128]{3,0,2,1:T(8,128)(2,1)S(1)} %get-tuple-element.236, bf16[8,512,2,128]{3,1,0,2:T(8,128)(2,1)} %get-tuple-element.235, s32[]{:T(128)S(6)} %copy.293), kind=kOutput, calls=%fused_computation.6.clone.1 | convolution fusion | flops 271579136 | bytes 5054468 | tf_op jit(solution)/shard_map/while/body/eval_jaxpr/qhgd,khd->hgqk/dot_general | solution.py:49
  286.3 3.3 %fusion.59 = f32[2,8,128]{2,1,0:T(8,128)S(1)} fusion(f32[2,512,128,8]{2,1,3,0:T(8,128)} %get-tuple-element.203, f32[2,8,128]{2,1,0:T(8,128)S(1)} %select_maximum_fusion.2, pred[128,512]{0,1:T(8,128)(4,1)S(1)} %broadcast_compare_fusion.2), kind=kLoop, calls=%fused_computation.8.clone.1 | loop fusion | flops 5240832 | bytes 4276224 | tf_op jit(solution)/shard_map/while/body/eval_jaxpr/reduce_sum | solution.py:58
  289.8 2.6 fusion.61
  293.9 3.6 %fusion.58 = (f32[2,8,128]{2,1,0:T(8,128)S(1)}, f32[2,512,128,8]{2,1,3,0:T(8,128)}) fusion(pred[128,512]{0,1:T(8,128)(4,1)S(1)} %broadcast_compare_fusion.2, bf16[128,2,8,128]{3,0,2,1:T(8,128)(2,1)S(1)} %get-tuple-element.236, bf16[8,512,2,128]{3,1,0,2:T(8,128)(2,1)} %get-tuple-element.235, s32[]{:T(128)S(6)} %copy.293), kind=kOutput, calls=%fused_computation.6.clone.1 | convolution fusion | flops 271579136 | bytes 5054468 | tf_op jit(solution)/shard_map/while/body/eval_jaxpr/qhgd,khd->hgqk/dot_general | solution.py:49
  297.5 3.3 %fusion.59 = f32[2,8,128]{2,1,0:T(8,128)S(1)} fusion(f32[2,512,128,8]{2,1,3,0:T(8,128)} %get-tuple-element.203, f32[2,8,128]{2,1,0:T(8,128)S(1)} %select_maximum_fusion.2, pred[128,512]{0,1:T(8,128)(4,1)S(1)} %broadcast_compare_fusion.2), kind=kLoop, calls=%fused_computation.8.clone.1 | loop fusion | flops 5240832 | bytes 4276224 | tf_op jit(solution)/shard_map/while/body/eval_jaxpr/reduce_sum | solution.py:58
  300.9 2.6 fusion.61
  305.0 3.6 %fusion.58 = (f32[2,8,128]{2,1,0:T(8,128)S(1)}, f32[2,512,128,8]{2,1,3,0:T(8,128)}) fusion(pred[128,512]{0,1:T(8,128)(4,1)S(1)} %broadcast_compare_fusion.2, bf16[128,2,8,128]{3,0,2,1:T(8,128)(2,1)S(1)} %get-tuple-element.236, bf16[8,512,2,128]{3,1,0,2:T(8,128)(2,1)} %get-tuple-element.235, s32[]{:T(128)S(6)} %copy.293), kind=kOutput, calls=%fused_computation.6.clone.1 | convolution fusion | flops 271579136 | bytes 5054468 | tf_op jit(solution)/shard_map/while/body/eval_jaxpr/qhgd,khd->hgqk/dot_general | solution.py:49
  308.6 3.3 %fusion.59 = f32[2,8,128]{2,1,0:T(8,128)S(1)} fusion(f32[2,512,128,8]{2,1,3,0:T(8,128)} %get-tuple-element.203, f32[2,8,128]{2,1,0:T(8,128)S(1)} %select_maximum_fusion.2, pred[128,512]{0,1:T(8,128)(4,1)S(1)} %broadcast_compare_fusion.2), kind=kLoop, calls=%fused_computation.8.clone.1 | loop fusion | flops 5240832 | bytes 4276224 | tf_op jit(solution)/shard_map/while/body/eval_jaxpr/reduce_sum | solution.py:58
  312.0 2.6 fusion.61
  318.3 2.3 multiply_reduce_fusion
  (177 shorter events, 41.4 us)
Async XLA Ops:
  7.2 148.7 %copy-start = (bf16[1024,128]{1,0:T(8,128)(2,1)S(1)}, bf16[1024,128]{1,0:T(8,128)(2,1)}, u32[]{:S(2)}) copy-start(bf16[1024,128]{1,0:T(8,128)(2,1)} %param.18) | copy-start | bytes 786436
  14.8 33.2 %copy-start.7 = (bf16[1,128,2,128]{3,2,1,0:T(2,128)(2,1)S(1)}, bf16[1,128,2,128]{3,2,1,0:T(2,128)(2,1)}, u32[]{:S(2)}) copy-start(bf16[1,128,2,128]{3,2,1,0:T(2,128)(2,1)} %param.14) | copy-start | bytes 196612
  34.7 41.3 %all-to-all-start = ((bf16[32,4,1,4,1024]{4,3,1,2,0:T(4,128)(2,1)}), bf16[32,4,1,4,1024]{4,3,1,2,0:T(4,128)(2,1)S(1)}, u32[]{:S(2)}, u32[]{:S(2)}) async-start(bf16[32,4,1,4,1024]{4,3,1,2,0:T(4,128)(2,1)} %constant_dynamic-update-slice_fusion), calls=%async_computation | async-start | bytes 2097152 | tf_op jit(solution)/shard_map/all_to_all | solution.py:122
  47.9 163.8 %all-gather.3.cloned.1.call-start = ((), (), s32[]{:S(2)}) async-start(), calls=%async_computation.4 | async-start | bytes 2162688 | tf_op jit(solution)/shard_map/all_gather | solution.py:37
  78.6 7.8 %copy-start.4 = (bf16[192,1024]{1,0:T(8,128)(2,1)S(1)}, bf16[192,1024]{1,0:T(8,128)(2,1)}, u32[]{:S(2)}) copy-start(bf16[192,1024]{1,0:T(8,128)(2,1)} %param.21) | copy-start | bytes 1179652
  78.6 7.8 %copy-start.5 = (bf16[192,1024]{1,0:T(8,128)(2,1)S(1)}, bf16[192,1024]{1,0:T(8,128)(2,1)}, u32[]{:S(2)}) copy-start(bf16[192,1024]{1,0:T(8,128)(2,1)} %param.20) | copy-start | bytes 1179652
  78.6 12.0 %copy-start.8 = (bf16[1,128,2,128]{3,2,1,0:T(2,128)(2,1)S(1)}, bf16[1,128,2,128]{3,2,1,0:T(2,128)(2,1)}, u32[]{:S(2)}) copy-start(bf16[1,128,2,128]{3,2,1,0:T(2,128)(2,1)} %param.15) | copy-start | bytes 196612
  78.6 55.1 %all-to-all-start.1 = ((bf16[16,16,4,1024]{3,2,1,0:T(4,128)(2,1)}), bf16[16,16,4,1024]{3,2,1,0:T(4,128)(2,1)S(1)}, u32[]{:S(2)}, u32[]{:S(2)}) async-start(bf16[16,16,4,1024]{3,2,1,0:T(4,128)(2,1)} %bitcast.312), calls=%async_computation.1 | async-start | bytes 4194304 | tf_op jit(solution)/shard_map/all_to_all | solution.py:140
  86.3 139.4 %all-gather.5.cloned.1.call-start = ((), (), s32[]{:S(2)}) async-start(), calls=%async_computation.5 | async-start | bytes 2162688 | tf_op jit(solution)/shard_map/all_gather | solution.py:38
  88.5 5.1 %collective-permute-start = (bf16[3,192,1024]{2,1,0:T(8,128)(2,1)}, bf16[3,192,1024]{2,1,0:T(8,128)(2,1)}, u32[]{:S(2)}, u32[]{:S(2)}) collective-permute-start(bf16[3,192,1024]{2,1,0:T(8,128)(2,1)} %pad_maximum_fusion), channel_id=1, source_target_pairs={{0,1},{1,0},{2,3},{3,2},{4,5},{5,4},{6,7},{7,6},{8,9},{9,8},{10,11... | collective-permute-start | bytes 3538952 | tf_op jit(solution)/shard_map/ppermute | solution.py:9
  135.8 3.2 copy-start.2
  135.8 3.2 copy-start.3
  147.3 8.1 %copy-start.9 = (s32[1,128,2]{1,2,0:T(2,128)S(1)}, s32[1,128,2]{1,2,0:T(2,128)}, u32[]{:S(2)}) copy-start(s32[1,128,2]{1,2,0:T(2,128)} %param.16) | copy-start | bytes 3076
  147.3 54.1 %all-to-all-start.2 = ((bf16[16,16,4,1024]{3,1,2,0:T(8,128)(2,1)}), bf16[16,16,4,1024]{3,1,2,0:T(8,128)(2,1)S(1)}, u32[]{:S(2)}, u32[]{:S(2)}) async-start(bf16[16,16,4,1024]{3,1,2,0:T(8,128)(2,1)} %convolution_convert_fusion), calls=%async_computation.2 | async-start | bytes 4194304 | tf_op jit(solution)/shard_map/all_to_all | solution.py:142
  204.5 21.2 %copy-start.6 = (f32[2,8,128,128]{3,2,1,0:T(8,128)S(1)}, f32[2,8,128,128]{3,2,1,0:T(8,128)}, u32[]{:S(2)}) copy-start(f32[2,8,128,128]{3,2,1,0:T(8,128)} %custom-call.4) | copy-start | bytes 3145732
  206.4 109.8 %all-to-all-start.3 = ((bf16[4,32,4,1024]{3,2,0,1:T(4,128)(2,1)}), bf16[4,32,4,1024]{3,2,0,1:T(4,128)(2,1)S(1)}, u32[]{:S(2)}, u32[]{:S(2)}) async-start(bf16[4,32,4,1024]{3,2,0,1:T(4,128)(2,1)} %copy.243), calls=%async_computation.3 | async-start | bytes 2097152 | tf_op jit(solution)/shard_map/all_to_all | solution.py:149
  230.7 3.4 %copy-start.1 = (f32[2,512,128,8]{2,1,3,0:T(8,128)S(1)}, f32[2,512,128,8]{2,1,3,0:T(8,128)}, u32[]{:S(2)}) copy-start(f32[2,512,128,8]{2,1,3,0:T(8,128)} %get-tuple-element.203) | copy-start | bytes 12582916 | tf_op jit(solution)/shard_map/while
  241.8 3.4 %copy-start.1 = (f32[2,512,128,8]{2,1,3,0:T(8,128)S(1)}, f32[2,512,128,8]{2,1,3,0:T(8,128)}, u32[]{:S(2)}) copy-start(f32[2,512,128,8]{2,1,3,0:T(8,128)} %get-tuple-element.203) | copy-start | bytes 12582916 | tf_op jit(solution)/shard_map/while
  252.9 3.4 %copy-start.1 = (f32[2,512,128,8]{2,1,3,0:T(8,128)S(1)}, f32[2,512,128,8]{2,1,3,0:T(8,128)}, u32[]{:S(2)}) copy-start(f32[2,512,128,8]{2,1,3,0:T(8,128)} %get-tuple-element.203) | copy-start | bytes 12582916 | tf_op jit(solution)/shard_map/while
  264.1 3.4 %copy-start.1 = (f32[2,512,128,8]{2,1,3,0:T(8,128)S(1)}, f32[2,512,128,8]{2,1,3,0:T(8,128)}, u32[]{:S(2)}) copy-start(f32[2,512,128,8]{2,1,3,0:T(8,128)} %get-tuple-element.203) | copy-start | bytes 12582916 | tf_op jit(solution)/shard_map/while
  275.2 3.4 %copy-start.1 = (f32[2,512,128,8]{2,1,3,0:T(8,128)S(1)}, f32[2,512,128,8]{2,1,3,0:T(8,128)}, u32[]{:S(2)}) copy-start(f32[2,512,128,8]{2,1,3,0:T(8,128)} %get-tuple-element.203) | copy-start | bytes 12582916 | tf_op jit(solution)/shard_map/while
  286.3 3.4 %copy-start.1 = (f32[2,512,128,8]{2,1,3,0:T(8,128)S(1)}, f32[2,512,128,8]{2,1,3,0:T(8,128)}, u32[]{:S(2)}) copy-start(f32[2,512,128,8]{2,1,3,0:T(8,128)} %get-tuple-element.203) | copy-start | bytes 12582916 | tf_op jit(solution)/shard_map/while
  297.5 3.4 %copy-start.1 = (f32[2,512,128,8]{2,1,3,0:T(8,128)S(1)}, f32[2,512,128,8]{2,1,3,0:T(8,128)}, u32[]{:S(2)}) copy-start(f32[2,512,128,8]{2,1,3,0:T(8,128)} %get-tuple-element.203) | copy-start | bytes 12582916 | tf_op jit(solution)/shard_map/while
  308.6 3.4 %copy-start.1 = (f32[2,512,128,8]{2,1,3,0:T(8,128)S(1)}, f32[2,512,128,8]{2,1,3,0:T(8,128)}, u32[]{:S(2)}) copy-start(f32[2,512,128,8]{2,1,3,0:T(8,128)} %get-tuple-element.203) | copy-start | bytes 12582916 | tf_op jit(solution)/shard_map/while
Sparse Core Ops, SparseCore 0:
  52.5 85.1 all-gather.2
  141.4 84.2 all-gather.4
